TPU v7x, 512 devices: a whole 4x8x8 slice. The times are simulated.
512 devices in a mesh: rx: 8 (over y), tm: 16 (over z, core), bin: 4 (over x).
Axes of the slice: x: 4, y: 8, z: 8, core: 2. Of those that a mesh axis runs over, the one named last changes fastest.
Arguments:
- samples: bfloat16 [4, 4096, 4096], P('bin', 'tm', 'rx'), may hold values from -45 to 45, as said below
- test_matrix: bfloat16 [4, 4096, 512], P('bin', 'tm'), may hold values from -0.09375 to 0.09375
- forgetting: float32 [4, 16, 512], P('bin', 'tm'), may hold values from 0 to 1, as said below
- prior_sketch: bfloat16 [4, 4096, 512], P('bin', 'rx'), may hold values from -6 to 6
Outputs:
- basis: bfloat16 [4, 16, 4096, 512], P('bin', 'tm', 'rx')
- coefficients: float32 [4, 4096, 512], P('bin', 'tm')
Inputs may be any that keep to these rules, and one draw needn't show every extreme that they name: `samples`: real-valued data. `forgetting`: positive factors.
All inputs are finite; a program needn't handle non-finite values.
Results may differ from a plain program's by a relative error of at most 0.015.
Values may be sent and summed in bfloat16 or wider, within the bound.
No kernel may reach another device: no remote copies, remote signals or barrier semaphores. Data moves between devices by JAX's collectives and lax.ppermute only.
A program may use at most 64 MiB of HBM per device.

v0:
```python
import math
import jax
import jax.numpy as jnp
from jax import lax
from jax.sharding import PartitionSpec as P


def prefix_2(part, axis, combine, identity):
    place = lax.axis_index(axis)
    gathered = jax.tree.map(lambda a: lax.all_gather(a, axis), part)
    state = jax.tree.map(lambda a, e: jnp.zeros_like(a) + jnp.asarray(e, a.dtype), part, identity)

    def one(hop, state):
        return combine(
            state, jax.tree.map(lambda a: lax.dynamic_index_in_dim(a, hop, 0, False), gathered)
        )

    return lax.fori_loop(0, place, one, state)


def with_halo(block, sides, width):
    for axis, dim in sides:
        count = lax.axis_size(axis)
        forward = [(i, i + 1) for i in range(count - 1)]
        backward = [(target, source) for source, target in forward]
        low = lax.ppermute(
            lax.slice_in_dim(block, block.shape[dim] - width, None, axis=dim), axis, forward
        )
        high = lax.ppermute(lax.slice_in_dim(block, 0, width, axis=dim), axis, backward)
        block = jnp.concatenate([low, block, high], axis=dim)
    return block


def combine(earlier, later):
    return (earlier[0] * later[0], later[0][None, :] * earlier[1] + later[1])


def sketch_of(block_data, block_test):
    return lax.dot_general(
        block_data, block_test, (((0,), (0,)), ((), ())), preferred_element_type=jnp.float32
    )


def body(samples, test_matrix, forgetting, prior_sketch):
    block_data = samples[0]
    block_test = test_matrix[0]
    own_decay = forgetting[0, 0]
    prior_rows = prior_sketch[0].astype(jnp.float32)
    width = block_test.shape[1]
    rows = block_data.shape[1]
    sketch = sketch_of(block_data, block_test)
    identity = (jnp.ones((width,), jnp.float32), jnp.zeros((rows, width), jnp.float32))
    before_decay, before_sum = prefix_2((own_decay, sketch), "tm", combine, identity)
    prefix = (
        own_decay[None, :] * before_sum + sketch + (before_decay * own_decay)[None, :] * prior_rows
    )
    padded = with_halo(prefix[None], (("bin", 0),), 1)
    mixed = padded[1] + 0.25 * (padded[0] + padded[2])
    local_gram = lax.dot_general(
        mixed,
        mixed,
        (((0,), (0,)), ((), ())),
        precision=lax.Precision.HIGHEST,
        preferred_element_type=jnp.float32,
    )
    gram = lax.psum(local_gram, "rx")
    factor = jnp.linalg.cholesky(gram)
    ortho = jax.scipy.linalg.solve_triangular(factor, mixed.T, lower=True).T
    local_coords = jnp.dot(
        block_data.astype(jnp.float32),
        ortho,
        precision=lax.Precision.HIGHEST,
        preferred_element_type=jnp.float32,
    )
    coords = lax.psum(local_coords.astype(jnp.bfloat16), "rx").astype(jnp.float32)
    receivers = rows * lax.axis_size("rx")
    basis = (math.sqrt(receivers) * ortho).astype(jnp.bfloat16)
    return (basis[None, None], coords[None])


def solution(mesh):
    return jax.shard_map(
        body,
        mesh=mesh,
        in_specs=(
            P("bin", "tm", "rx"),
            P("bin", "tm", None),
            P("bin", "tm", None),
            P("bin", "rx", None),
        ),
        out_specs=(P("bin", "tm", "rx", None), P("bin", "tm", None)),
        check_vma=False,
    )
```

profile of v0, /device:TPU:2, one launch (start us, length us, event | category | flops | bytes accessed | tf_op | source)
XLA Modules:
  0.0 489.7 jit_solution(11235781154400756800)
XLA Ops:
  7.2 0.9 copy-done
  8.1 2.3 fusion.15
  10.5 23.6 %all-gather = f32[16,1,512]{2,1,0:T(1,128)S(1)} all-gather(f32[1,1,512]{2,1,0:T(1,128)} %param.8), channel_id=2, replica_groups=mesh['rx'=8,'tm'=16,'bin'=4] {'tm'}, dimensions={0}, use_global_device_ids=true | all-gather | bytes 34816 | tf_op jit(solution)/shard_map/all_gather | solution.py:10
  34.1 79.9 %all-gather.4.cloned.1.call-done = f32[8192,512]{1,0:T(8,128)} async-done(((f32[512,512]{1,0:T(8,128)}), f32[8192,512]{1,0:T(8,128)}) %all-gather.4.cloned.1.call-update) | async-done | bytes 16777232 | tf_op jit(solution)/shard_map/all_gather | solution.py:10
  114.5 3.4 collective-permute-start
  117.9 2.5 collective-permute-start.1
  120.4 21.0 %collective-permute-done = f32[1,512,512]{2,1,0:T(8,128)S(1)} collective-permute-done((f32[1,512,512]{2,1,0:T(8,128)S(1)}, f32[1,512,512]{2,1,0:T(8,128)S(1)}, u32[]{:S(2)}, u32[]{:S(2)}) %collective-permute-start) | collective-permute-done | bytes 1048608 | tf_op jit(solution)/shard_map/ppermute | solution.py:26
  141.4 3.7 collective-permute-done.1
  145.1 1.6 bitcast_add_fusion.2
  146.7 2.9 fusion.40
  149.6 0.5 all-reduce.6.cloned.1.call-start
  150.1 101.0 %all-reduce.4.cloned.1.call-done = f32[512,512]{0,1:T(8,128)} async-done(((f32[512,512]{0,1:T(8,128)}), f32[512,512]{0,1:T(8,128)}) %all-reduce.4.cloned.1.call-update) | async-done | bytes 1048592 | tf_op jit(solution)/shard_map/psum | solution.py:66
  251.1 1.6 copy.12
  252.7 1.4 fusion.2
  254.2 11.7 %cholesky.103 = f32[128,128]{1,0:T(8,128)S(1)} custom-call(f32[128,128]{1,0:T(8,128)S(1)} %cholesky.263), custom_call_target="Cholesky" | custom-call | tf_op jit(solution)/shard_map/jit(cholesky)/cholesky | solution.py:67
  266.0 9.8 %custom-call.31 = f32[1,128,128]{1,2,0:T(8,128)S(1)} custom-call(f32[1,128,128]{2,1,0:T(8,128)S(1)} %get-tuple-element.81), custom_call_target="InvertDiagBlocksLowerTriangular" | custom-call | tf_op jit(solution)/shard_map/jit(cholesky)/cholesky | solution.py:67
  276.5 0.7 copy-done.3
  277.2 11.7 %cholesky.215 = f32[128,128]{1,0:T(8,128)S(1)} custom-call(f32[128,128]{1,0:T(8,128)S(1)} %cholesky.267), custom_call_target="Cholesky" | custom-call | tf_op jit(solution)/shard_map/jit(cholesky)/cholesky | solution.py:67
  288.9 10.0 %custom-call.32 = f32[1,128,128]{1,2,0:T(8,128)S(1)} custom-call(f32[1,128,128]{2,1,0:T(8,128)S(1)} %get-tuple-element.78), custom_call_target="InvertDiagBlocksLowerTriangular" | custom-call | tf_op jit(solution)/shard_map/jit(cholesky)/cholesky | solution.py:67
  298.9 1.2 convolution_dynamic-update-slice_fusion
  300.5 0.6 cholesky.272
  301.1 13.2 %cholesky.236 = f32[128,128]{1,0:T(8,128)} custom-call(f32[128,128]{1,0:T(8,128)} %cholesky.272), custom_call_target="Cholesky" | custom-call | tf_op jit(solution)/shard_map/jit(cholesky)/cholesky | solution.py:67
  314.3 1.5 select_reduce_fusion.1
  315.8 0.7 compare_reduce_fusion.1
  316.4 11.3 %custom-call.33 = f32[1,128,128]{1,2,0:T(8,128)} custom-call(f32[1,128,128]{2,1,0:T(8,128)} %get-tuple-element.75), custom_call_target="InvertDiagBlocksLowerTriangular" | custom-call | tf_op jit(solution)/shard_map/jit(cholesky)/cholesky | solution.py:67
  327.7 1.0 convolution_dynamic-update-slice_fusion.1
  329.1 11.7 %cholesky.253 = f32[128,128]{1,0:T(8,128)S(1)} custom-call(f32[128,128]{1,0:T(8,128)S(1)} %convolution_subtract_fusion.5), custom_call_target="Cholesky" | custom-call | tf_op jit(solution)/shard_map/jit(cholesky)/cholesky | solution.py:67
  340.9 0.7 compare_reduce_fusion
  341.6 0.6 compare_reduce_fusion.2
  345.1 10.9 %while.14 = (s32[]{:T(128)}, f32[512,512]{1,0:T(8,128)S(1)}, s32[4,2]{0,1:T(2,128)S(1)}, f32[4,128,128]{2,1,0:T(8,128)}, s32[]{:T(128)}) while((s32[]{:T(128)}, f32[512,512]{1,0:T(8,128)S(1)}, s32[4,2]{0,1:T(2,128)S(1)}, f32[4,128,128]{2,1,0:T(8,128)}, s32[]{:T(128)}) %tuple.49), condition=%wide.while_cond, body=%wide.while_body.sunk | while | flops 2 | bytes 132705 | solution.py:68
  345.2 0.6 fusion.49
  345.8 2.1 bitcast_dynamic-update-slice_fusion.2
  347.9 0.6 fusion.49
  348.5 2.1 bitcast_dynamic-update-slice_fusion.2
  350.6 0.6 fusion.49
  351.2 2.1 bitcast_dynamic-update-slice_fusion.2
  353.4 0.6 fusion.49
  354.0 2.1 bitcast_dynamic-update-slice_fusion.2
  356.0 40.1 %custom-call.34 = f32[4,128,128]{1,2,0:T(8,128)S(1)} custom-call(f32[4,128,128]{2,1,0:T(8,128)} %get-tuple-element.45), custom_call_target="InvertDiagBlocksLowerTriangular" | custom-call | tf_op jit(solution)/shard_map/jit(_solve_triangular)/triangular_solve | solution.py:68
  396.6 0.6 convolution_subtract_fusion.1
  397.6 1.0 convolution_subtract_fusion
  398.6 1.3 fusion.27
  399.9 1.5 convolution_subtract_fusion.2
  401.4 1.3 fusion.26
  402.6 1.3 fusion
  404.1 1.0 copy.13
  405.1 75.9 %all-reduce.6.cloned.1.call-done = bf16[1,256,512]{1,2,0:T(8,128)(2,1)} async-done(((bf16[1,256,512]{1,2,0:T(8,128)(2,1)}), bf16[1,256,512]{1,2,0:T(8,128)(2,1)}) %all-reduce.6.cloned.1.call-update) | async-done | bytes 262160 | tf_op jit(solution)/shard_map/psum | solution.py:75
  481.0 1.9 copy.14
  (42 shorter events, 3.8 us)
Async XLA Ops:
  7.2 1.0 copy-start
  7.2 107.0 %copy-start.5 = (f32[1,1,512]{2,1,0:T(1,128)S(1)}, f32[1,1,512]{2,1,0:T(1,128)}, u32[]{:S(2)}) copy-start(f32[1,1,512]{2,1,0:T(1,128)} %param.8) | copy-start | bytes 6148
  7.2 107.0 %copy-start.2 = (bf16[1,512,512]{2,1,0:T(8,128)(2,1)S(1)}, bf16[1,512,512]{2,1,0:T(8,128)(2,1)}, u32[]{:S(2)}) copy-start(bf16[1,512,512]{2,1,0:T(8,128)(2,1)} %param.9) | copy-start | bytes 1572868
  7.2 106.8 %all-gather.4.cloned.1.call-start = ((), (), s32[]{:S(2)}) async-start(), calls=%async_computation.2 | async-start | bytes 17825792 | tf_op jit(solution)/shard_map/all_gather | solution.py:10
  10.4 103.8 %copy-start.1 = (f32[512,512]{1,0:T(8,128)S(1)}, f32[512,512]{1,0:T(8,128)}, u32[]{:S(2)}) copy-start(f32[512,512]{1,0:T(8,128)} %fusion.15) | copy-start | bytes 3145732
  10.4 240.7 %all-reduce.4.cloned.1.call-start = ((), (), s32[]{:S(2)}) async-start(), calls=%async_computation | async-start | bytes 2097152 | tf_op jit(solution)/shard_map/psum | solution.py:66
  114.5 27.0 %collective-permute-start = (f32[1,512,512]{2,1,0:T(8,128)S(1)}, f32[1,512,512]{2,1,0:T(8,128)S(1)}, u32[]{:S(2)}, u32[]{:S(2)}) collective-permute-start(f32[1,512,512]{2,1,0:T(8,128)S(1)} %fusion.35), channel_id=1, source_target_pairs={{0,1},{1,2},{2,3},{4,5},{5,6},{6,7},{8,9},{9,10},{10,11},{12,13},{... | collective-permute-start | bytes 3145736 | tf_op jit(solution)/shard_map/ppermute | solution.py:26
  117.9 27.2 %collective-permute-start.1 = (f32[1,512,512]{2,1,0:T(8,128)S(1)}, f32[1,512,512]{2,1,0:T(8,128)S(1)}, u32[]{:S(2)}, u32[]{:S(2)}) collective-permute-start(f32[1,512,512]{2,1,0:T(8,128)S(1)} %fusion.35), channel_id=1, source_target_pairs={{1,0},{2,1},{3,2},{5,4},{6,5},{7,6},{9,8},{10,9},{11,10},{13,12},{... | collective-permute-start | bytes 3145736 | tf_op jit(solution)/shard_map/ppermute | solution.py:29
  149.6 331.4 %all-reduce.6.cloned.1.call-start = ((), (), s32[]{:S(2)}) async-start(), calls=%async_computation.1 | async-start | bytes 524288 | tf_op jit(solution)/shard_map/psum | solution.py:75
  276.5 0.7 copy-start.3
  396.1 1.1 copy-start.4
Sparse Core Ops, SparseCore 0:
  10.5 103.3 all-gather.3
  149.7 101.3 all-reduce.3
  404.1 76.8 all-reduce.5
where the time goes:
time: 495 us; the launch traced here: 490 us
  waiting for transfers between devices  282 us (57%)
  other arithmetic  127 us (26%)
  blocking collectives  23.6 us (5%)
  local copies, waits for them, and re-layouts  17.8 us (4%)
  between operations  16.8 us (3%)
  matrix products  16.5 us (3%)
  starting transfers between devices  6.49 us (1%)
    psum x1, waiting for transfers between devices, body(): gram = lax.psum(local_gram, 'rx')  101 us
    another operation x14, other arithmetic, body(): factor = jnp.linalg.cholesky(gram)  82.9 us
    all_gather x1, waiting for transfers between devices, prefix_2(): gathered = jax.tree.map(lambda a: lax.all_gather(a, axis), part)  79.9 us
    psum x1, waiting for transfers between devices, body(): lax.psum(local_coords.astype(jnp.bfloat16), 'rx').astype(jnp.float32)  75.9 us
    another operation x3, other arithmetic, body(): ortho = jax.scipy.linalg.solve_triangular(factor, mixed.T, lower=True).T  40.4 us
    all_gather x1, blocking collectives, prefix_2(): gathered = jax.tree.map(lambda a: lax.all_gather(a, axis), part)  23.6 us
    ppermute x1, waiting for transfers between devices, with_halo(): lax.ppermute(lax.slice_in_dim(block, block.shape[dim] - width, None, axis...  21 us
    another operation x12, local copies, waits for them, and re-layouts  10.9 us
  transfers between devices with their start and end apart: 5, of which 5 were waited for; matrix products, arithmetic and copies ran while one was open for 0% of the time, Pallas kernels for 0%

commit v1 on v0

--- a/solution.py
+++ b/solution.py
@@ -72,7 +72,9 @@
         precision=lax.Precision.HIGHEST,
         preferred_element_type=jnp.float32,
     )
-    coords = lax.psum(local_coords.astype(jnp.bfloat16), "rx").astype(jnp.float32)
+    coords = jnp.sum(lax.all_gather(local_coords.astype(jnp.bfloat16), "rx"), axis=0).astype(
+        jnp.float32
+    )
     receivers = rows * lax.axis_size("rx")
     basis = (math.sqrt(receivers) * ortho).astype(jnp.bfloat16)
     return (basis[None, None], coords[None])

time: 495 us -> 464 us (0.937)
  waiting for transfers between devices: 282 us -> 253 us
  other arithmetic: 127 us -> 122 us
    psum x1 -> x0, waiting for transfers between devices: 75.9 us -> none  [body(): lax.psum(local_coords.astype(jnp.bfloat16), 'rx').astype(jnp.float32)]
    all_gather x0 -> x1, waiting for transfers between devices: none -> 47.9 us  [body(): lax.all_gather(local_coords.astype(jnp.bfloat16), 'rx')]
where the time goes in v1:
time: 464 us; the launch traced here: 460 us
  waiting for transfers between devices  253 us (55%)
  other arithmetic  122 us (26%)
  blocking collectives  23.2 us (5%)
  local copies, waits for them, and re-layouts  19.9 us (4%)
  matrix products  18.4 us (4%)
  between operations  16.9 us (4%)
  starting transfers between devices  6.49 us (1%)
    psum x1, waiting for transfers between devices, body(): gram = lax.psum(local_gram, 'rx')  99.6 us
    all_gather x1, waiting for transfers between devices, prefix_2(): gathered = jax.tree.map(lambda a: lax.all_gather(a, axis), part)  80.3 us
    another operation x14, other arithmetic, body(): factor = jnp.linalg.cholesky(gram)  78.7 us
    all_gather x1, waiting for transfers between devices, body(): lax.all_gather(local_coords.astype(jnp.bfloat16), 'rx')  47.9 us
    another operation x3, other arithmetic, body(): ortho = jax.scipy.linalg.solve_triangular(factor, mixed.T, lower=True).T  40.4 us
    all_gather x1, blocking collectives, prefix_2(): gathered = jax.tree.map(lambda a: lax.all_gather(a, axis), part)  23.2 us
    ppermute x1, waiting for transfers between devices, with_halo(): lax.ppermute(lax.slice_in_dim(block, block.shape[dim] - width, None, axis...  21.8 us
    another operation x12, local copies, waits for them, and re-layouts  10.6 us
  transfers between devices with their start and end apart: 5, of which 5 were waited for; matrix products, arithmetic and copies ran while one was open for 0% of the time, Pallas kernels for 0%

profile of v1, /device:TPU:2, one launch (start us, length us, event | category | flops | bytes accessed | tf_op | source)
XLA Modules:
  0.0 459.6 jit_solution(7548295647289480427)
XLA Ops:
  7.2 0.9 copy-done
  8.1 2.3 fusion.15
  10.5 23.2 %all-gather = f32[16,1,512]{2,1,0:T(1,128)S(1)} all-gather(f32[1,1,512]{2,1,0:T(1,128)S(1)} %copy-done.7), channel_id=2, replica_groups=mesh['rx'=8,'tm'=16,'bin'=4] {'tm'}, dimensions={0}, use_global_device_ids=true | all-gather | bytes 34816 | tf_op jit(solution)/shard_map/all_gather | solution.py:10
  33.7 80.3 %all-gather.6.cloned.1.call-done = f32[8192,512]{1,0:T(8,128)} async-done(((f32[512,512]{1,0:T(8,128)}), f32[8192,512]{1,0:T(8,128)}) %all-gather.6.cloned.1.call-update) | async-done | bytes 16777232 | tf_op jit(solution)/shard_map/all_gather | solution.py:10
  114.2 1.2 copy-done.1
  115.8 3.4 collective-permute-start
  119.1 2.5 collective-permute-start.1
  121.7 21.8 %collective-permute-done = f32[1,512,512]{2,1,0:T(8,128)S(1)} collective-permute-done((f32[1,512,512]{2,1,0:T(8,128)S(1)}, f32[1,512,512]{2,1,0:T(8,128)S(1)}, u32[]{:S(2)}, u32[]{:S(2)}) %collective-permute-start) | collective-permute-done | bytes 1048608 | tf_op jit(solution)/shard_map/ppermute | solution.py:26
  143.5 3.1 collective-permute-done.1
  147.2 2.9 fusion.40
  150.6 99.6 %all-reduce.3.cloned.1.call-done = f32[512,512]{0,1:T(8,128)} async-done(((f32[512,512]{0,1:T(8,128)}), f32[512,512]{0,1:T(8,128)}) %all-reduce.3.cloned.1.call-update) | async-done | bytes 1048592 | tf_op jit(solution)/shard_map/psum | solution.py:66
  250.2 1.6 copy.11
  252.1 1.0 copy-done.3
  253.1 11.7 %cholesky.103 = f32[128,128]{1,0:T(8,128)S(1)} custom-call(f32[128,128]{1,0:T(8,128)S(1)} %cholesky.263), custom_call_target="Cholesky" | custom-call | tf_op jit(solution)/shard_map/jit(cholesky)/cholesky | solution.py:67
  265.0 9.8 %custom-call.31 = f32[1,128,128]{1,2,0:T(8,128)S(1)} custom-call(f32[1,128,128]{2,1,0:T(8,128)S(1)} %get-tuple-element.81), custom_call_target="InvertDiagBlocksLowerTriangular" | custom-call | tf_op jit(solution)/shard_map/jit(cholesky)/cholesky | solution.py:67
  274.8 1.2 constant_dynamic-update-slice_fusion.3
  276.0 1.3 convolution_subtract_fusion.3
  277.3 11.7 %cholesky.215 = f32[128,128]{1,0:T(8,128)S(1)} custom-call(f32[128,128]{1,0:T(8,128)S(1)} %cholesky.267), custom_call_target="Cholesky" | custom-call | tf_op jit(solution)/shard_map/jit(cholesky)/cholesky | solution.py:67
  289.0 10.0 %custom-call.32 = f32[1,128,128]{1,2,0:T(8,128)S(1)} custom-call(f32[1,128,128]{2,1,0:T(8,128)S(1)} %get-tuple-element.78), custom_call_target="InvertDiagBlocksLowerTriangular" | custom-call | tf_op jit(solution)/shard_map/jit(cholesky)/cholesky | solution.py:67
  299.3 1.3 convolution_subtract_fusion.4
  300.6 11.7 %cholesky.236 = f32[128,128]{1,0:T(8,128)S(1)} custom-call(f32[128,128]{1,0:T(8,128)S(1)} %cholesky.272), custom_call_target="Cholesky" | custom-call | tf_op jit(solution)/shard_map/jit(cholesky)/cholesky | solution.py:67
  312.3 0.7 compare_reduce_fusion.1
  313.1 9.8 %custom-call.33 = f32[1,128,128]{1,2,0:T(8,128)S(1)} custom-call(f32[1,128,128]{2,1,0:T(8,128)S(1)} %get-tuple-element.75), custom_call_target="InvertDiagBlocksLowerTriangular" | custom-call | tf_op jit(solution)/shard_map/jit(cholesky)/cholesky | solution.py:67
  323.1 1.2 convolution_subtract_fusion.5
  324.3 11.7 %cholesky.253 = f32[128,128]{1,0:T(8,128)S(1)} custom-call(f32[128,128]{1,0:T(8,128)S(1)} %convolution_subtract_fusion.5), custom_call_target="Cholesky" | custom-call | tf_op jit(solution)/shard_map/jit(cholesky)/cholesky | solution.py:67
  336.0 0.7 compare_reduce_fusion
  336.8 0.7 compare_reduce_fusion.2
  340.4 10.6 %while.14 = (s32[]{:T(128)}, f32[512,512]{1,0:T(8,128)S(1)}, s32[4,2]{0,1:T(2,128)S(1)}, f32[4,128,128]{2,1,0:T(8,128)}, s32[]{:T(128)}) while((s32[]{:T(128)}, f32[512,512]{1,0:T(8,128)S(1)}, s32[4,2]{0,1:T(2,128)S(1)}, f32[4,128,128]{2,1,0:T(8,128)}, s32[]{:T(128)}) %tuple.49), condition=%wide.while_cond, body=%wide.while_body.sunk | while | flops 2 | bytes 132705 | solution.py:68
  340.4 0.6 fusion.49
  341.0 2.0 bitcast_dynamic-update-slice_fusion.2
  343.1 0.6 fusion.49
  343.7 2.0 bitcast_dynamic-update-slice_fusion.2
  345.7 0.6 fusion.49
  346.3 2.0 bitcast_dynamic-update-slice_fusion.2
  348.4 0.6 fusion.49
  349.0 2.0 bitcast_dynamic-update-slice_fusion.2
  351.0 40.1 %custom-call.34 = f32[4,128,128]{1,2,0:T(8,128)S(1)} custom-call(f32[4,128,128]{2,1,0:T(8,128)} %get-tuple-element.45), custom_call_target="InvertDiagBlocksLowerTriangular" | custom-call | tf_op jit(solution)/shard_map/jit(_solve_triangular)/triangular_solve | solution.py:68
  391.5 0.6 convolution_subtract_fusion.1
  392.6 1.0 convolution_subtract_fusion
  393.6 1.3 fusion.27
  394.8 1.5 convolution_subtract_fusion.2
  396.3 1.3 fusion.26
  397.6 1.3 fusion
  399.1 1.0 copy.12
  400.1 47.9 %all-gather.8.cloned.1.call-done = bf16[2048,512]{0,1:T(8,128)(2,1)} async-done(((bf16[256,512]{0,1:T(8,128)(2,1)}), bf16[2048,512]{0,1:T(8,128)(2,1)}) %all-gather.8.cloned.1.call-update) | async-done | bytes 2097168 | tf_op jit(solution)/shard_map/all_gather | solution.py:75
  448.0 2.3 copy.16
  450.3 1.5 bitcast_reduce_fusion
  451.9 1.0 copy.13
  (49 shorter events, 4.4 us)
Async XLA Ops:
  7.2 1.0 copy-start
  7.2 3.3 copy-start.7
  7.2 106.8 %all-gather.6.cloned.1.call-start = ((), (), s32[]{:S(2)}) async-start(), calls=%async_computation.1 | async-start | bytes 17825792 | tf_op jit(solution)/shard_map/all_gather | solution.py:10
  10.4 239.8 %all-reduce.3.cloned.1.call-start = ((), (), s32[]{:S(2)}) async-start(), calls=%async_computation | async-start | bytes 2097152 | tf_op jit(solution)/shard_map/psum | solution.py:66
  114.1 1.2 copy-start.1
  114.1 1.3 copy-start.4
  114.2 32.5 %copy-start.5 = (bf16[1,512,512]{2,1,0:T(8,128)(2,1)S(1)}, bf16[1,512,512]{2,1,0:T(8,128)(2,1)}, u32[]{:S(2)}) copy-start(bf16[1,512,512]{2,1,0:T(8,128)(2,1)} %param.9) | copy-start | bytes 1572868
  115.8 27.7 %collective-permute-start = (f32[1,512,512]{2,1,0:T(8,128)S(1)}, f32[1,512,512]{2,1,0:T(8,128)S(1)}, u32[]{:S(2)}, u32[]{:S(2)}) collective-permute-start(f32[1,512,512]{2,1,0:T(8,128)S(1)} %fusion.35), channel_id=1, source_target_pairs={{0,1},{1,2},{2,3},{4,5},{5,6},{6,7},{8,9},{9,10},{10,11},{12,13},{... | collective-permute-start | bytes 3145736 | tf_op jit(solution)/shard_map/ppermute | solution.py:26
  119.1 27.5 %collective-permute-start.1 = (f32[1,512,512]{2,1,0:T(8,128)S(1)}, f32[1,512,512]{2,1,0:T(8,128)S(1)}, u32[]{:S(2)}, u32[]{:S(2)}) collective-permute-start(f32[1,512,512]{2,1,0:T(8,128)S(1)} %fusion.35), channel_id=1, source_target_pairs={{1,0},{2,1},{3,2},{5,4},{6,5},{7,6},{9,8},{10,9},{11,10},{13,12},{... | collective-permute-start | bytes 3145736 | tf_op jit(solution)/shard_map/ppermute | solution.py:29
  150.1 297.9 %all-gather.8.cloned.1.call-start = ((), (), s32[]{:S(2)}) async-start(), calls=%async_computation.2 | async-start | bytes 2359296 | tf_op jit(solution)/shard_map/all_gather | solution.py:75
  250.2 1.7 copy-start.2
  252.1 1.0 copy-start.3
  391.1 1.1 copy-start.6
Sparse Core Ops, SparseCore 0:
  10.5 103.3 all-gather.5
  150.2 99.9 all-reduce.2
  399.1 48.8 all-gather.7
